TPU v7x, 128 devices: a whole 4x4x4 slice. The times are simulated.
128 devices in a mesh: row: 16 (over x, y_hi, core), col: 8 (over z, y_lo).
Axes of the slice: x: 4, y: 4 (y_hi: 2, y_lo: 2; y = y_hi * 2 + y_lo), z: 4, core: 2. Of those that a mesh axis runs over, the one named last changes fastest.
Arguments:
- band_cells: float32 [3, 1024, 2], P(None, ('row', 'col')), may hold values from 0 to 1
- cell_counts: int32 [1024], P(('row', 'col')), may hold values from 1 to 2, as said below
- cell_assign: int32 [1024], P(('row', 'col')), may hold values from 0 to 1023, as said below
- wake_pos: float32 [3, 1048576], P(None, ('row', 'col')), may hold values from 0 to 1
- wake_strength: float32 [3, 1048576], P(None, ('row', 'col')), may hold values from -0.005859375 to 0.005859375
- wake_core: float32 [1, 1048576], P(None, ('row', 'col')), may hold values from 0.05 to 0.15
Outputs:
- velocity: float32 [3, 1024, 2], P(None, ('row', 'col'))
- gradient: float32 [9, 1024, 2], P(None, ('row', 'col'))
Inputs may be any that keep to these rules, and one draw needn't show every extreme that they name: `cell_counts`: each band cell holds its live particles in its first slots; some cell is full in every draw. `cell_assign`: A permutation of the cells. The cells of the device with index d along row+col go to positions q with q // 64 == d // 8; at most 1 of them land in the positions of any one device (q // 8); where 8 is a multiple of 8, exactly 1 land in the positions of each device of the group, else some pair of devices reaches 1.
All inputs are finite; a program needn't handle non-finite values.
Results may differ from a plain program's by a relative error of at most 0.0003.
Values sent between devices are 32-bit elements; how exact they have to be, the bound alone decides.
No kernel may reach another device: no remote copies, remote signals or barrier semaphores. Data moves between devices by JAX's collectives and lax.ppermute only.
A program may use at most 64 MiB of HBM per device.

v0:
```python
import math
import jax
import jax.numpy as jnp
from jax import lax
from jax.sharding import PartitionSpec as P

HIGHEST = lax.Precision.HIGHEST


def block_sums(target_pos, source_pos, source_str, source_core):
    delta_x = target_pos[0][:, None] - source_pos[0][None, :]
    delta_y = target_pos[1][:, None] - source_pos[1][None, :]
    delta_z = target_pos[2][:, None] - source_pos[2][None, :]
    radius_sq = (
        delta_x * delta_x
        + delta_y * delta_y
        + delta_z * delta_z
        + source_core[0][None, :] * source_core[0][None, :]
    )
    inverse = lax.rsqrt(radius_sq)
    kernel_three = inverse * inverse * inverse
    kernel_five = kernel_three * inverse * inverse
    alpha_x = source_str[0][None, :]
    alpha_y = source_str[1][None, :]
    alpha_z = source_str[2][None, :]
    cross_x = delta_y * alpha_z - delta_z * alpha_y
    cross_y = delta_z * alpha_x - delta_x * alpha_z
    cross_z = delta_x * alpha_y - delta_y * alpha_x
    terms_list = [
        kernel_three * cross_x,
        kernel_three * cross_y,
        kernel_three * cross_z,
        kernel_three * alpha_x,
        kernel_three * alpha_y,
        kernel_three * alpha_z,
    ]
    for along in (delta_x, delta_y, delta_z):
        for cross in (cross_x, cross_y, cross_z):
            terms_list.append(kernel_five * along * cross)
    return jnp.stack([jnp.sum(term, axis=1) for term in terms_list])


def pair_sums(target_pos, source_pos, source_str, source_core):
    source_total = source_pos.shape[1]
    block_width = math.gcd(source_total, max(512, 1048576 // target_pos.shape[1]))
    block_steps = source_total // block_width

    def one_block(running, block_index):
        offset = block_index * block_width
        part_pos = lax.dynamic_slice_in_dim(source_pos, offset, block_width, 1)
        part_str = lax.dynamic_slice_in_dim(source_str, offset, block_width, 1)
        part_core = lax.dynamic_slice_in_dim(source_core, offset, block_width, 1)
        return (running + block_sums(target_pos, part_pos, part_str, part_core), None)

    start_sums = jnp.zeros((15, target_pos.shape[1]), jnp.float32)
    running, unused = lax.scan(one_block, start_sums, jnp.arange(block_steps, dtype=jnp.int32))
    return running


def combine_rows(kernel_sums):
    biot_scale = -1.0 / (4.0 * math.pi)
    swirl_x, swirl_y, swirl_z = (kernel_sums[3], kernel_sums[4], kernel_sums[5])
    zero_row = jnp.zeros_like(swirl_x)
    levi_terms = [
        [zero_row, swirl_z, -swirl_y],
        [-swirl_z, zero_row, swirl_x],
        [swirl_y, -swirl_x, zero_row],
    ]
    out_rows = [
        biot_scale * kernel_sums[0],
        biot_scale * kernel_sums[1],
        biot_scale * kernel_sums[2],
    ]
    for comp_m in range(3):
        for comp_n in range(3):
            out_rows.append(
                biot_scale
                * (levi_terms[comp_m][comp_n] - 3.0 * kernel_sums[6 + comp_n * 3 + comp_m])
            )
    return jnp.stack(out_rows)


def apply_mask(finished_rows, slot_counts, slot_cap):
    slot_ids = jnp.arange(slot_cap).astype(slot_counts.dtype)
    alive_mask = (slot_ids[None, :] < slot_counts[:, None]).astype(jnp.float32).reshape(-1)
    masked = finished_rows * alive_mask[None, :]
    cell_total = slot_counts.shape[0]
    return (
        masked[0:3].reshape(3, cell_total, slot_cap),
        masked[3:12].reshape(9, cell_total, slot_cap),
    )


def per_device(band_cells, cell_counts, cell_assign, wake_pos, wake_strength, wake_core):
    axes = ("row", "col")
    col_devs = lax.axis_size("col")
    cell_total = band_cells.shape[1]
    slot_cap = band_cells.shape[2]
    group_cells = cell_total * col_devs
    packed = jnp.concatenate(
        [
            band_cells.transpose(1, 0, 2).reshape(cell_total, 3 * slot_cap),
            cell_counts.astype(jnp.float32)[:, None],
            cell_assign.astype(jnp.float32)[:, None],
        ],
        axis=1,
    )
    every_cell = lax.all_gather(packed, axes, axis=0, tiled=True)
    all_cells = every_cell.shape[0]
    groups = all_cells // group_cells
    grouped = every_cell.reshape(groups, group_cells, 3 * slot_cap + 2)
    within = grouped[:, :, -1].astype(jnp.int32) % group_cells
    position = jnp.arange(group_cells, dtype=jnp.int32)
    chosen = within[:, None, :] == position[None, :, None]
    relaid = jnp.sum(
        jnp.where(chosen[:, :, :, None], grouped[:, None, :, : 3 * slot_cap + 1], 0.0), axis=2
    ).reshape(all_cells, 3 * slot_cap + 1)
    target_pos = relaid[:, : 3 * slot_cap].reshape(all_cells, 3, slot_cap)
    target_pos = target_pos.transpose(1, 0, 2).reshape(3, all_cells * slot_cap)
    device = lax.axis_index("row") * col_devs + lax.axis_index("col")
    own_counts = lax.dynamic_slice_in_dim(relaid[:, 3 * slot_cap], device * cell_total, cell_total)
    local_sums = pair_sums(target_pos, wake_pos, wake_strength, wake_core)
    own_rows = lax.psum_scatter(local_sums, axes, scatter_dimension=1, tiled=True)
    finished_rows = combine_rows(own_rows)
    return apply_mask(finished_rows, own_counts, slot_cap)


def solution(mesh):
    placed = (
        P(None, ("row", "col"), None),
        P(("row", "col")),
        P(("row", "col")),
        P(None, ("row", "col")),
        P(None, ("row", "col")),
        P(None, ("row", "col")),
    )
    return jax.shard_map(
        per_device,
        mesh=mesh,
        in_specs=placed,
        out_specs=(P(None, ("row", "col"), None), P(None, ("row", "col"), None)),
        check_vma=False,
    )
```

profile of v0, /device:TPU:0, one launch (start us, length us, event | category | flops | bytes accessed | tf_op | source)
XLA Modules:
  0.0 1217.7 jit_solution(9751047633105874884)
XLA Ops:
  7.2 0.7 reshape.74
  7.9 0.7 convert_bitcast_fusion
  8.7 320.8 %all_gather.3 = f32[1024,8]{1,0:T(8,128)S(1)} all-gather(f32[8,8]{1,0:T(8,128)S(1)} %copy.62), channel_id=1, replica_groups=mesh['row'=16,'col'=8] {'row','col'}, dimensions={0}, use_global_device_ids=true | all-gather | bytes 33024 | tf_op jit(solution)/shard_map/all_gather | solution.py:108
  330.2 1.0 select_reduce_fusion
  331.9 0.9 reshape.78
  332.8 240.7 %while.11 = (s32[]{:T(128)}, f32[15,2048]{1,0:T(8,128)S(1)}, f32[3,2048]{1,0:T(4,128)S(1)}, s32[16]{0:T(128)S(1)}, f32[3,8192]{1,0:T(4,128)}, /*index=5*/f32[1,8...) while((s32[]{:T(128)}, f32[15,2048]{1,0:T(8,128)S(1)}, ...), condition=%wide.region_17.18_spmd.clone, body=%wide.region_1.17_spmd.clone.sunk | while | flops 57702920 | bytes 854257 | solution.py:56
  332.8 0.6 dynamic_slice.24
  334.1 0.9 constant_dynamic-slice_fusion.3
  334.9 0.9 fusion.55
  335.9 11.7 fusion.57
  349.1 0.9 constant_dynamic-slice_fusion.3
  350.0 0.9 fusion.55
  350.9 11.7 fusion.57
  362.9 0.6 dynamic_slice.24
  364.1 0.9 constant_dynamic-slice_fusion.3
  365.0 0.9 fusion.55
  365.9 11.7 fusion.57
  377.9 0.6 dynamic_slice.24
  379.2 0.9 constant_dynamic-slice_fusion.3
  380.1 0.9 fusion.55
  381.0 11.7 fusion.57
  393.0 0.6 dynamic_slice.24
  394.2 0.9 constant_dynamic-slice_fusion.3
  395.1 0.9 fusion.55
  396.0 11.7 fusion.57
  408.0 0.6 dynamic_slice.24
  409.3 0.9 constant_dynamic-slice_fusion.3
  410.2 0.9 fusion.55
  411.1 11.7 fusion.57
  424.3 0.9 constant_dynamic-slice_fusion.3
  425.2 0.9 fusion.55
  426.1 11.7 fusion.57
  439.3 0.9 constant_dynamic-slice_fusion.3
  440.2 0.9 fusion.55
  441.2 11.7 fusion.57
  454.4 0.9 constant_dynamic-slice_fusion.3
  455.3 0.9 fusion.55
  456.2 11.7 fusion.57
  469.4 0.9 constant_dynamic-slice_fusion.3
  470.3 0.9 fusion.55
  471.2 11.7 fusion.57
  484.5 0.9 constant_dynamic-slice_fusion.3
  485.4 0.9 fusion.55
  486.3 11.7 fusion.57
  499.5 0.9 constant_dynamic-slice_fusion.3
  500.4 0.9 fusion.55
  501.3 11.7 fusion.57
  514.6 0.9 constant_dynamic-slice_fusion.3
  515.5 0.9 fusion.55
  516.4 11.7 fusion.57
  529.6 0.9 constant_dynamic-slice_fusion.3
  530.5 0.9 fusion.55
  531.4 11.7 fusion.57
  544.6 0.9 constant_dynamic-slice_fusion.3
  545.5 0.9 fusion.55
  546.5 11.7 fusion.57
  559.7 0.9 constant_dynamic-slice_fusion.3
  560.6 0.9 fusion.55
  561.5 11.7 fusion.57
  573.5 1.4 copy.84
  575.1 632.5 %reduce-scatter.4.cloned.1.call-done = f32[16,15]{1,0:T(8,128)} async-done(((f32[2048,15]{1,0:T(8,128)}), f32[16,15]{1,0:T(8,128)}) %reduce-scatter.4.cloned.1.call-update) | async-done | bytes 976
  1207.6 1.7 fusion.33
  1209.5 0.7 slice.140
  1210.2 0.7 copy.83
  (81 shorter events, 12.5 us)
Async XLA Ops:
  7.2 1200.5 %reduce-scatter.4.cloned.1.call-start = ((), (), s32[]{:S(2)}) async-start(), calls=%async_computation.1 | async-start | bytes 1056768
Sparse Core Ops, SparseCore 0:
  575.0 632.5 reduce-scatter.3
where the time goes:
time: 1220 us
  waiting for transfers between devices  633 us (52%)
  blocking collectives  321 us (26%)
  other arithmetic  206 us (17%)
  local copies, waits for them, and re-layouts  33 us (3%)
  between operations  14.1 us (1%)
    unnamed x2, waiting for transfers between devices  633 us
    all_gather x1, blocking collectives, per_device(): every_cell = lax.all_gather(packed, axes, axis=0, tiled=True)  321 us
    reduce_sum x16, other arithmetic, block_sums(): return jnp.stack([jnp.sum(term, axis=1) for term in terms_list])  187 us
  transfers between devices with their start and end apart: 1, of which 1 were waited for; matrix products, arithmetic and copies ran while one was open for 0% of the time, Pallas kernels for 0%

commit v1 on v0

--- a/solution.py
+++ b/solution.py
@@ -105,7 +105,10 @@
         ],
         axis=1,
     )
-    every_cell = lax.all_gather(packed, axes, axis=0, tiled=True)
+    n_dev = lax.axis_size(axes)
+    blocks = jnp.stack([packed for _ in range(n_dev)])
+    blocks = lax.all_to_all(blocks, axes, split_axis=0, concat_axis=0)
+    every_cell = jnp.concatenate(blocks, axis=0)
     all_cells = every_cell.shape[0]
     groups = all_cells // group_cells
     grouped = every_cell.reshape(groups, group_cells, 3 * slot_cap + 2)

time: 1220 us -> 926 us (0.76)
  blocking collectives: 321 us -> 0 us
  waiting for transfers between devices: 633 us -> 648 us
    all_gather x1 -> x0, blocking collectives: 321 us -> none  [per_device(): every_cell = lax.all_gather(packed, axes, axis=0, tiled=True)]
    all_to_all x0 -> x1, waiting for transfers between devices: none -> 13.7 us  [per_device(): blocks = lax.all_to_all(blocks, axes, split_axis=0, concat_axis=0)]
  transfers between devices with their start and end apart: 1 -> 2, of which waited for: 1 -> 2; matrix products, arithmetic and copies ran while one was open for 0% -> 0% of each run, Pallas kernels for 0% -> 0%
where the time goes in v1:
time: 926 us; the launch traced here: 924 us
  waiting for transfers between devices  648 us (70%)
  other arithmetic  206 us (22%)
  local copies, waits for them, and re-layouts  33.5 us (4%)
  between operations  14.1 us (2%)
  starting transfers between devices  11.2 us (1%)
  loops' own time  11.1 us (1%)
    unnamed x2, waiting for transfers between devices  635 us
    reduce_sum x16, other arithmetic, block_sums(): return jnp.stack([jnp.sum(term, axis=1) for term in terms_list])  187 us
  transfers between devices with their start and end apart: 2, of which 2 were waited for; matrix products, arithmetic and copies ran while one was open for 0% of the time, Pallas kernels for 0%

profile of v1, /device:TPU:0, one launch (start us, length us, event | category | flops | bytes accessed | tf_op | source)
XLA Modules:
  0.0 924.3 jit_solution(3807354312942650091)
XLA Ops:
  7.2 0.7 reshape.73
  7.9 0.7 convert_bitcast_fusion
  8.5 0.8 stack.36
  9.4 11.1 %all-to-all-start = ((f32[128,8,8]{1,2,0:T(8,128)}), f32[128,8,8]{1,2,0:T(8,128)S(1)}, u32[]{:S(2)}, u32[]{:S(2)}) async-start(f32[128,8,8]{1,2,0:T(8,128)} %stack.36), calls=%async_computation | async-start | bytes 1048576 | tf_op jit(solution)/shard_map/all_to_all | solution.py:110
  20.6 13.7 %all-to-all-done = f32[128,8,8]{1,2,0:T(8,128)S(1)} async-done(((f32[128,8,8]{1,2,0:T(8,128)}), f32[128,8,8]{1,2,0:T(8,128)S(1)}, u32[]{:S(2)}, u32[]{:S(2)}) %all-to-all-start) | async-done | bytes 32800 | tf_op jit(solution)/shard_map/all_to_all | solution.py:110
  34.7 1.0 select_reduce_fusion
  36.4 0.9 reshape.76
  37.3 240.7 %while.11 = (s32[]{:T(128)}, f32[15,2048]{1,0:T(8,128)S(1)}, f32[3,2048]{1,0:T(4,128)S(1)}, s32[16]{0:T(128)S(1)}, f32[3,8192]{1,0:T(4,128)}, /*index=5*/f32[1,8...) while((s32[]{:T(128)}, f32[15,2048]{1,0:T(8,128)S(1)}, ...), condition=%wide.region_17.18_spmd.clone, body=%wide.region_1.17_spmd.clone.sunk | while | flops 57702920 | bytes 854257 | solution.py:56
  38.5 0.9 constant_dynamic-slice_fusion.3
  39.4 0.9 fusion.56
  40.4 11.7 %fusion.58 = (f32[2048]{0:T(1024)S(1)}, f32[2048]{0:T(1024)S(1)}, f32[2048]{0:T(1024)S(1)}, f32[2048]{0:T(1024)S(1)}, f32[2048]{0:T(1024)S(1)}, /*index=5*/f32[2...) fusion(f32[512]{0:T(512)S(1)} %bitcast.135, ...), kind=kLoop, calls=%fused_computation.28.clone.1 | loop fusion | flops 57640960 | bytes 161792 | tf_op jit(solution)/shard_map/while/body/eval_jaxpr/reduce_sum | solution.py:40
  52.3 0.6 dynamic_slice.24
  53.6 0.9 constant_dynamic-slice_fusion.3
  54.5 0.9 fusion.56
  55.4 11.7 %fusion.58 = (f32[2048]{0:T(1024)S(1)}, f32[2048]{0:T(1024)S(1)}, f32[2048]{0:T(1024)S(1)}, f32[2048]{0:T(1024)S(1)}, f32[2048]{0:T(1024)S(1)}, /*index=5*/f32[2...) fusion(f32[512]{0:T(512)S(1)} %bitcast.135, ...), kind=kLoop, calls=%fused_computation.28.clone.1 | loop fusion | flops 57640960 | bytes 161792 | tf_op jit(solution)/shard_map/while/body/eval_jaxpr/reduce_sum | solution.py:40
  67.4 0.6 dynamic_slice.24
  68.6 0.9 constant_dynamic-slice_fusion.3
  69.5 0.9 fusion.56
  70.4 11.7 %fusion.58 = (f32[2048]{0:T(1024)S(1)}, f32[2048]{0:T(1024)S(1)}, f32[2048]{0:T(1024)S(1)}, f32[2048]{0:T(1024)S(1)}, f32[2048]{0:T(1024)S(1)}, /*index=5*/f32[2...) fusion(f32[512]{0:T(512)S(1)} %bitcast.135, ...), kind=kLoop, calls=%fused_computation.28.clone.1 | loop fusion | flops 57640960 | bytes 161792 | tf_op jit(solution)/shard_map/while/body/eval_jaxpr/reduce_sum | solution.py:40
  82.4 0.6 dynamic_slice.24
  83.7 0.9 constant_dynamic-slice_fusion.3
  84.6 0.9 fusion.56
  85.5 11.7 %fusion.58 = (f32[2048]{0:T(1024)S(1)}, f32[2048]{0:T(1024)S(1)}, f32[2048]{0:T(1024)S(1)}, f32[2048]{0:T(1024)S(1)}, f32[2048]{0:T(1024)S(1)}, /*index=5*/f32[2...) fusion(f32[512]{0:T(512)S(1)} %bitcast.135, ...), kind=kLoop, calls=%fused_computation.28.clone.1 | loop fusion | flops 57640960 | bytes 161792 | tf_op jit(solution)/shard_map/while/body/eval_jaxpr/reduce_sum | solution.py:40
  98.7 0.9 constant_dynamic-slice_fusion.3
  99.6 0.9 fusion.56
  100.5 11.7 %fusion.58 = (f32[2048]{0:T(1024)S(1)}, f32[2048]{0:T(1024)S(1)}, f32[2048]{0:T(1024)S(1)}, f32[2048]{0:T(1024)S(1)}, f32[2048]{0:T(1024)S(1)}, /*index=5*/f32[2...) fusion(f32[512]{0:T(512)S(1)} %bitcast.135, ...), kind=kLoop, calls=%fused_computation.28.clone.1 | loop fusion | flops 57640960 | bytes 161792 | tf_op jit(solution)/shard_map/while/body/eval_jaxpr/reduce_sum | solution.py:40
  113.8 0.9 constant_dynamic-slice_fusion.3
  114.7 0.9 fusion.56
  115.6 11.7 %fusion.58 = (f32[2048]{0:T(1024)S(1)}, f32[2048]{0:T(1024)S(1)}, f32[2048]{0:T(1024)S(1)}, f32[2048]{0:T(1024)S(1)}, f32[2048]{0:T(1024)S(1)}, /*index=5*/f32[2...) fusion(f32[512]{0:T(512)S(1)} %bitcast.135, ...), kind=kLoop, calls=%fused_computation.28.clone.1 | loop fusion | flops 57640960 | bytes 161792 | tf_op jit(solution)/shard_map/while/body/eval_jaxpr/reduce_sum | solution.py:40
  128.8 0.9 constant_dynamic-slice_fusion.3
  129.7 0.9 fusion.56
  130.6 11.7 %fusion.58 = (f32[2048]{0:T(1024)S(1)}, f32[2048]{0:T(1024)S(1)}, f32[2048]{0:T(1024)S(1)}, f32[2048]{0:T(1024)S(1)}, f32[2048]{0:T(1024)S(1)}, /*index=5*/f32[2...) fusion(f32[512]{0:T(512)S(1)} %bitcast.135, ...), kind=kLoop, calls=%fused_computation.28.clone.1 | loop fusion | flops 57640960 | bytes 161792 | tf_op jit(solution)/shard_map/while/body/eval_jaxpr/reduce_sum | solution.py:40
  143.8 0.9 constant_dynamic-slice_fusion.3
  144.7 0.9 fusion.56
  145.7 11.7 %fusion.58 = (f32[2048]{0:T(1024)S(1)}, f32[2048]{0:T(1024)S(1)}, f32[2048]{0:T(1024)S(1)}, f32[2048]{0:T(1024)S(1)}, f32[2048]{0:T(1024)S(1)}, /*index=5*/f32[2...) fusion(f32[512]{0:T(512)S(1)} %bitcast.135, ...), kind=kLoop, calls=%fused_computation.28.clone.1 | loop fusion | flops 57640960 | bytes 161792 | tf_op jit(solution)/shard_map/while/body/eval_jaxpr/reduce_sum | solution.py:40
  158.9 0.9 constant_dynamic-slice_fusion.3
  159.8 0.9 fusion.56
  160.7 11.7 %fusion.58 = (f32[2048]{0:T(1024)S(1)}, f32[2048]{0:T(1024)S(1)}, f32[2048]{0:T(1024)S(1)}, f32[2048]{0:T(1024)S(1)}, f32[2048]{0:T(1024)S(1)}, /*index=5*/f32[2...) fusion(f32[512]{0:T(512)S(1)} %bitcast.135, ...), kind=kLoop, calls=%fused_computation.28.clone.1 | loop fusion | flops 57640960 | bytes 161792 | tf_op jit(solution)/shard_map/while/body/eval_jaxpr/reduce_sum | solution.py:40
  173.9 0.9 constant_dynamic-slice_fusion.3
  174.8 0.9 fusion.56
  175.7 11.7 %fusion.58 = (f32[2048]{0:T(1024)S(1)}, f32[2048]{0:T(1024)S(1)}, f32[2048]{0:T(1024)S(1)}, f32[2048]{0:T(1024)S(1)}, f32[2048]{0:T(1024)S(1)}, /*index=5*/f32[2...) fusion(f32[512]{0:T(512)S(1)} %bitcast.135, ...), kind=kLoop, calls=%fused_computation.28.clone.1 | loop fusion | flops 57640960 | bytes 161792 | tf_op jit(solution)/shard_map/while/body/eval_jaxpr/reduce_sum | solution.py:40
  189.0 0.9 constant_dynamic-slice_fusion.3
  189.9 0.9 fusion.56
  190.8 11.7 %fusion.58 = (f32[2048]{0:T(1024)S(1)}, f32[2048]{0:T(1024)S(1)}, f32[2048]{0:T(1024)S(1)}, f32[2048]{0:T(1024)S(1)}, f32[2048]{0:T(1024)S(1)}, /*index=5*/f32[2...) fusion(f32[512]{0:T(512)S(1)} %bitcast.135, ...), kind=kLoop, calls=%fused_computation.28.clone.1 | loop fusion | flops 57640960 | bytes 161792 | tf_op jit(solution)/shard_map/while/body/eval_jaxpr/reduce_sum | solution.py:40
  204.0 0.9 constant_dynamic-slice_fusion.3
  204.9 0.9 fusion.56
  205.8 11.7 %fusion.58 = (f32[2048]{0:T(1024)S(1)}, f32[2048]{0:T(1024)S(1)}, f32[2048]{0:T(1024)S(1)}, f32[2048]{0:T(1024)S(1)}, f32[2048]{0:T(1024)S(1)}, /*index=5*/f32[2...) fusion(f32[512]{0:T(512)S(1)} %bitcast.135, ...), kind=kLoop, calls=%fused_computation.28.clone.1 | loop fusion | flops 57640960 | bytes 161792 | tf_op jit(solution)/shard_map/while/body/eval_jaxpr/reduce_sum | solution.py:40
  219.1 0.9 constant_dynamic-slice_fusion.3
  219.9 0.9 fusion.56
  220.9 11.7 %fusion.58 = (f32[2048]{0:T(1024)S(1)}, f32[2048]{0:T(1024)S(1)}, f32[2048]{0:T(1024)S(1)}, f32[2048]{0:T(1024)S(1)}, f32[2048]{0:T(1024)S(1)}, /*index=5*/f32[2...) fusion(f32[512]{0:T(512)S(1)} %bitcast.135, ...), kind=kLoop, calls=%fused_computation.28.clone.1 | loop fusion | flops 57640960 | bytes 161792 | tf_op jit(solution)/shard_map/while/body/eval_jaxpr/reduce_sum | solution.py:40
  234.1 0.9 constant_dynamic-slice_fusion.3
  235.0 0.9 fusion.56
  235.9 11.7 %fusion.58 = (f32[2048]{0:T(1024)S(1)}, f32[2048]{0:T(1024)S(1)}, f32[2048]{0:T(1024)S(1)}, f32[2048]{0:T(1024)S(1)}, f32[2048]{0:T(1024)S(1)}, /*index=5*/f32[2...) fusion(f32[512]{0:T(512)S(1)} %bitcast.135, ...), kind=kLoop, calls=%fused_computation.28.clone.1 | loop fusion | flops 57640960 | bytes 161792 | tf_op jit(solution)/shard_map/while/body/eval_jaxpr/reduce_sum | solution.py:40
  249.1 0.9 constant_dynamic-slice_fusion.3
  250.0 0.9 fusion.56
  250.9 11.7 %fusion.58 = (f32[2048]{0:T(1024)S(1)}, f32[2048]{0:T(1024)S(1)}, f32[2048]{0:T(1024)S(1)}, f32[2048]{0:T(1024)S(1)}, f32[2048]{0:T(1024)S(1)}, /*index=5*/f32[2...) fusion(f32[512]{0:T(512)S(1)} %bitcast.135, ...), kind=kLoop, calls=%fused_computation.28.clone.1 | loop fusion | flops 57640960 | bytes 161792 | tf_op jit(solution)/shard_map/while/body/eval_jaxpr/reduce_sum | solution.py:40
  264.2 0.9 constant_dynamic-slice_fusion.3
  265.1 0.9 fusion.56
  266.0 11.7 %fusion.58 = (f32[2048]{0:T(1024)S(1)}, f32[2048]{0:T(1024)S(1)}, f32[2048]{0:T(1024)S(1)}, f32[2048]{0:T(1024)S(1)}, f32[2048]{0:T(1024)S(1)}, /*index=5*/f32[2...) fusion(f32[512]{0:T(512)S(1)} %bitcast.135, ...), kind=kLoop, calls=%fused_computation.28.clone.1 | loop fusion | flops 57640960 | bytes 161792 | tf_op jit(solution)/shard_map/while/body/eval_jaxpr/reduce_sum | solution.py:40
  278.0 1.4 copy.86
  279.6 634.6 %reduce-scatter.4.cloned.1.call-done = f32[16,15]{1,0:T(8,128)} async-done(((f32[2048,15]{1,0:T(8,128)}), f32[16,15]{1,0:T(8,128)}) %reduce-scatter.4.cloned.1.call-update) | async-done | bytes 976
  914.2 1.7 fusion.33
  916.1 0.7 slice.140
  916.8 0.7 copy.85
  (83 shorter events, 13.3 us)
Async XLA Ops:
  9.4 24.9 %all-to-all-start = ((f32[128,8,8]{1,2,0:T(8,128)}), f32[128,8,8]{1,2,0:T(8,128)S(1)}, u32[]{:S(2)}, u32[]{:S(2)}) async-start(f32[128,8,8]{1,2,0:T(8,128)} %stack.36), calls=%async_computation | async-start | bytes 1048576 | tf_op jit(solution)/shard_map/all_to_all | solution.py:110
  20.5 893.7 %reduce-scatter.4.cloned.1.call-start = ((), (), s32[]{:S(2)}) async-start(), calls=%async_computation.2 | async-start | bytes 1056768
Sparse Core Ops, SparseCore 0:
  279.5 634.6 reduce-scatter.3
